TPU v7x, 512 devices: a whole 4x8x8 slice. The times are simulated.
512 devices in a mesh: ctx: 64 (over z, y), section: 2 (over x_hi), dp: 4 (over x_lo, core).
Axes of the slice: x: 4 (x_hi: 2, x_lo: 2; x = x_hi * 2 + x_lo), y: 8, z: 8, core: 2. Of those that a mesh axis runs over, the one named last changes fastest.
Arguments:
- query_vectors: bfloat16 [4, 8192, 1792], P('dp', 'ctx', 'section'), may hold values from -16 to 16
- key_vectors: bfloat16 [4, 8192, 256], P('dp', 'ctx', 'section'), may hold values from -16 to 16
- value_vectors: bfloat16 [4, 8192, 256], P('dp', 'ctx', 'section'), may hold values from -6 to 6
- grad_output: bfloat16 [4, 8192, 1792], P('dp', 'ctx', 'section'), may hold values from -24 to 24
- output_dots: float32 [4, 14, 8192], P('dp', 'section', 'ctx'), may hold values from -12 to 12
- frame_ids: int32 [4, 8192], P('dp'), may hold values from 0 to 63, never falling along the last dimension, each value on 1 to 256 neighbouring positions
- visual_rows: int32 [4, 64, 32], P('dp', 'ctx'), may hold values from 0 to 127, as said below
- shuffle_source: int32 [4, 128, 64], P('dp', ('ctx', 'section')), may hold values from 0 to 63, each once within a row
- qkv_weight: bfloat16 [2304, 3584], P(None, ('section', 'dp')), may hold values from -0.125 to 0.125
- projector_weight: bfloat16 [3584, 2560], P(('section', 'dp')), may hold values from -0.09375 to 0.09375
Outputs:
- grad_keys: bfloat16 [4, 8192, 256], P('dp', 'ctx', 'section')
- grad_values: bfloat16 [4, 8192, 256], P('dp', 'ctx', 'section')
- patch_grads: bfloat16 [4, 8192, 640], P('dp', ('ctx', 'section'))
Inputs may be any that keep to these rules, and one draw needn't show every extreme that they name: `frame_ids`: frame numbers never fall along a sequence; a frame holds 1 to 256 tokens. `visual_rows`: each block of 128 tokens lists 32 distinct positions in increasing order. `shuffle_source`: each row is a permutation.
All inputs are finite; a program needn't handle non-finite values.
Results may differ from a plain program's by a relative error of at most 0.014.
Values may be sent and summed in bfloat16 or wider, within the bound.
No kernel may reach another device: no remote copies, remote signals or barrier semaphores. Data moves between devices by JAX's collectives and lax.ppermute only.
A program may use at most 128 MiB of HBM per device.

v0:
```python
import math
import jax
import jax.numpy as jnp
from jax import lax
from jax.sharding import PartitionSpec as P

HEAD_DIM = 128
GROUP = 7
MASKED = -1e30


def shards(
    query_vectors,
    key_vectors,
    value_vectors,
    grad_output,
    output_dots,
    frame_ids,
    visual_rows,
    shuffle_source,
    qkv_weight,
    projector_weight,
):
    ring_z = lax.axis_size("cz")
    ring_y = lax.axis_size("cy")
    position = lax.axis_index("cz") * ring_y + lax.axis_index("cy")
    local_rows = query_vectors.shape[1]
    scale_factor = 1.0 / math.sqrt(HEAD_DIM)
    query_heads = query_vectors[0].reshape(local_rows, GROUP, HEAD_DIM)
    grad_heads = grad_output[0].reshape(local_rows, GROUP, HEAD_DIM)
    corrections = output_dots[0]
    frame_line = frame_ids[0]
    seq_total = frame_line.shape[0]
    query_first = position * local_rows
    query_pos = query_first + jnp.arange(local_rows, dtype=jnp.int32)
    query_frames = lax.dynamic_slice_in_dim(frame_line, query_first, local_rows)
    own_pair = jnp.concatenate([key_vectors[0], value_vectors[0]], axis=1)
    all_pairs = lax.all_gather(
        lax.all_to_all(jnp.tile(own_pair, (ring_z, 1)), "cz", 0, 0, tiled=True),
        "cy",
        axis=0,
        tiled=True,
    )
    key_all = all_pairs[:, :HEAD_DIM]
    value_all = all_pairs[:, HEAD_DIM:]
    key_pos = (
        jnp.arange(seq_total, dtype=jnp.int32)
        .reshape(ring_z, ring_y, local_rows)
        .transpose(1, 0, 2)
        .reshape(seq_total)
    )
    key_frames = (
        frame_line.reshape(ring_z, ring_y, local_rows).transpose(1, 0, 2).reshape(seq_total)
    )
    allowed = (key_pos[None, :] <= query_pos[:, None]) | (
        key_frames[None, :] == query_frames[:, None]
    )
    scores = (
        jnp.einsum("qhd,kd->hqk", query_heads, key_all, preferred_element_type=jnp.float32)
        * scale_factor
    )
    masked_scores = jnp.where(allowed[None], scores, MASKED)
    running = masked_scores.max(axis=-1)
    summed = jnp.exp(masked_scores - running[:, :, None]).sum(axis=-1)
    log_total = running + jnp.log(summed)
    probability = jnp.exp(jnp.where(allowed[None], scores - log_total[:, :, None], MASKED))
    probs_low = probability.astype(jnp.bfloat16)
    grad_probs = jnp.einsum(
        "qhd,kd->hqk", grad_heads, value_all, preferred_element_type=jnp.float32
    )
    grad_scores = (probability * (grad_probs - corrections[:, :, None])).astype(jnp.bfloat16)
    grad_query = (
        jnp.einsum("hqk,kd->qhd", grad_scores, key_all, preferred_element_type=jnp.float32)
        * scale_factor
    )
    key_part = (
        jnp.einsum("hqk,qhd->kd", grad_scores, query_heads, preferred_element_type=jnp.float32)
        * scale_factor
    )
    value_part = jnp.einsum(
        "hqk,qhd->kd", probs_low, grad_heads, preferred_element_type=jnp.float32
    )
    stage_one = lax.psum_scatter(
        jnp.concatenate([key_part, value_part], axis=1).astype(jnp.bfloat16),
        "cy",
        scatter_dimension=0,
        tiled=True,
    )
    stage_two = lax.all_to_all(stage_one, "cz", 0, 0, tiled=True)
    summed_grads = (
        stage_two.astype(jnp.float32).reshape(ring_z, local_rows, stage_two.shape[1]).sum(0)
    )
    grad_keys_low = summed_grads[:, :HEAD_DIM].astype(jnp.bfloat16)
    grad_values_low = summed_grads[:, HEAD_DIM:].astype(jnp.bfloat16)
    grad_query_low = grad_query.astype(jnp.bfloat16).reshape(local_rows, GROUP * HEAD_DIM)
    visual_picks = visual_rows[0, 0]
    chosen = jnp.concatenate(
        [grad_query_low[visual_picks], grad_keys_low[visual_picks], grad_values_low[visual_picks]],
        axis=1,
    )
    everyone = lax.all_gather(chosen[None], ("section", "dp"), axis=0, tiled=True)
    groups = lax.axis_size("section")
    replicas = lax.axis_size("dp")
    half_rows = visual_picks.shape[0] // 2
    width_in = chosen.shape[1]
    arranged = (
        everyone.reshape(groups, replicas, 2, half_rows, width_in)
        .transpose(2, 1, 3, 0, 4)
        .reshape(2 * replicas * half_rows, groups * width_in)
    )
    visual_grad = jnp.dot(arranged, qkv_weight, preferred_element_type=jnp.float32).astype(
        jnp.bfloat16
    )
    pieces = lax.all_to_all(
        jnp.dot(visual_grad, projector_weight, preferred_element_type=jnp.float32).astype(
            jnp.bfloat16
        ),
        ("section", "dp"),
        0,
        0,
        tiled=True,
    )
    shuffled = pieces.astype(jnp.float32).reshape(groups * replicas, -1, pieces.shape[1]).sum(0)
    slot_rows = shuffled.reshape(half_rows * 4, projector_weight.shape[1] // 4)
    patches = slot_rows[shuffle_source[0, 0]].astype(jnp.bfloat16)
    return (grad_keys_low[None], grad_values_low[None], patches[None])


def solution(mesh):
    ctx_size = mesh.shape["ctx"]
    ring_y = 8 if ctx_size % 8 == 0 else 1
    split_mesh = jax.sharding.Mesh(
        mesh.devices.reshape(ctx_size // ring_y, ring_y, mesh.shape["section"], mesh.shape["dp"]),
        ("cz", "cy", "section", "dp"),
    )
    ctx = ("cz", "cy")
    placed = (
        P("dp", ctx, "section"),
        P("dp", ctx, "section"),
        P("dp", ctx, "section"),
        P("dp", ctx, "section"),
        P("dp", "section", ctx),
        P("dp", None),
        P("dp", ctx, None),
        P("dp", ("cz", "cy", "section"), None),
        P(None, ("section", "dp")),
        P(("section", "dp"), None),
    )
    return jax.shard_map(
        shards,
        mesh=split_mesh,
        in_specs=placed,
        out_specs=(
            P("dp", ctx, "section"),
            P("dp", ctx, "section"),
            P("dp", ("cz", "cy", "section"), None),
        ),
        check_vma=False,
    )
```

profile of v0, /device:TPU:1, one launch (start us, length us, event | category | flops | bytes accessed | tf_op | source)
XLA Modules:
  0.0 288.4 jit_solution(3191562445234428152)
XLA Ops:
  7.2 0.0 copy-start
  7.2 0.0 all-gather.3.cloned.1.call-start
  7.2 0.9 pad_maximum_fusion.2
  8.2 26.8 %all_to_all.27 = bf16[8,128,256]{2,1,0:T(8,128)(2,1)} all-to-all(bf16[8,128,256]{2,1,0:T(8,128)(2,1)S(1)} %tile.2), channel_id=1, replica_groups=mesh['cz'=8,'cy'=8,'section'=2,'dp'=4] {'cz'}, dimensions={0} | all-to-all | bytes 1048576 | tf_op jit(solution)/shard_map/all_to_all | solution.py:39
  35.0 0.0 all-gather.3.cloned.1.call-update
  35.0 0.0 reduce-scatter.2.cloned.1.call-start
  35.0 1.8 copy.46
  36.8 1.8 copy.44
  38.6 0.7 copy.74
  39.3 0.7 dynamic-slice_bitcast_fusion
  39.9 0.8 copy_bitcast_fusion.1
  40.7 2.8 compare_or_fusion
  43.5 46.8 %all-gather.3.cloned.1.call-done = bf16[8192,256]{1,0:T(8,128)(2,1)} async-done(((bf16[1024,256]{1,0:T(8,128)(2,1)}), bf16[8192,256]{1,0:T(8,128)(2,1)}) %all-gather.3.cloned.1.call-update) | async-done | bytes 4194320 | tf_op jit(solution)/shard_map/all_gather | solution.py:38
  90.2 13.1 %fusion.4 = (f32[7,128]{1,0:T(8,128)S(1)}, f32[8192,128,7]{1,0,2:T(8,128)}) fusion(pred[128,8192]{0,1:T(8,128)(4,1)S(1)} %compare_or_fusion, bf16[128,7,128]{0,2,1:T(8,128)(2,1)} %bitcast.113, bf16[8192,256]{1,0:T(8,128)(2,1)} %all-gather.3.cloned.1.call-done), kind=kOutput, calls=%fused_computation.12 | convolution fusion | flops 1901067392 | bytes 32738816 | tf_op jit(solution)/shard_map/qhd,kd->hqk/dot_general | solution.py:59
  103.4 12.7 %exponential_reduce_fusion = f32[7,128]{1,0:T(8,128)S(1)} fusion(f32[8192,128,7]{1,0,2:T(8,128)} %get-tuple-element.6, f32[7,128]{1,0:T(8,128)S(1)} %get-tuple-element.5, pred[128,8192]{0,1:T(8,128)(4,1)S(1)} %compare_or_fusion), kind=kLoop, calls=%fused_computation.11 | loop fusion | flops 29359232 | bytes 30415872 | tf_op jit(solution)/shard_map/reduce_sum | solution.py:64
  116.1 0.0 copy-done.4
  116.1 0.0 copy-start.1
  116.1 13.4 %fusion.13 = bf16[8192,128]{0,1:T(8,128)(2,1)S(1)} fusion(bf16[128,7,128]{0,2,1:T(8,128)(2,1)S(1)} %bitcast.111, f32[8192,128,7]{1,0,2:T(8,128)} %get-tuple-element.6, f32[7,128]{1,0:T(8,128)S(1)} %log_add_fusion, pred[128,8192]{0,1:T(8,128)(4,1)S(1)} %compare_or_fusion), kind=kOutput, calls=%fused_computation.19 | convolution fusion | flops 1909456896 | bytes 32738816 | tf_op jit(solution)/shard_map/hqk,qhd->kd/dot_general | solution.py:80
  129.5 0.0 copy-done.1
  129.5 19.4 %fusion.1 = bf16[7,128,8192]{1,2,0:T(8,128)(2,1)} fusion(f32[8192,128,7]{1,0,2:T(8,128)} %get-tuple-element.6, bf16[128,7,128]{0,2,1:T(8,128)(2,1)S(1)} %bitcast.112, f32[7,128]{1,0:T(8,128)S(1)} %bitcast.119, f32[7,128]{1,0:T(8,128)S(1)} %log_add_fusion, pred[128,8192]{0,1:T(8,128)(4,1)S(1)} %compare_or_fusion, bf16[8192,256]{1,0:T(8,128)(2,1)S(1)} %copy-done.1), kind=kOutput, calls=%fused_computation.6 | convolution fusion | flops 1923088384 | bytes 47423488 | tf_op jit(solution)/shard_map/qhd,kd->hqk/dot_general | solution.py:68
  148.9 9.9 %fusion.16 = bf16[8192,128]{0,1:T(8,128)(2,1)S(1)} fusion(bf16[7,128,8192]{1,2,0:T(8,128)(2,1)} %fusion.1, bf16[128,7,128]{0,2,1:T(8,128)(2,1)S(1)} %bitcast.114), kind=kOutput, calls=%fused_computation.20 | convolution fusion | flops 1881145344 | bytes 17006592 | tf_op jit(solution)/shard_map/hqk,qhd->kd/dot_general | solution.py:77
  158.8 0.0 copy-start.6
  158.8 2.4 pad_maximum_fusion
  161.2 0.0 reduce-scatter.2.cloned.1.call-update
  161.3 56.8 %reduce-scatter.2.cloned.1.call-done = bf16[1024,256]{0,1:T(8,128)(2,1)} async-done(((bf16[8192,256]{0,1:T(8,128)(2,1)}), bf16[1024,256]{0,1:T(8,128)(2,1)}) %reduce-scatter.2.cloned.1.call-update) | async-done | bytes 524304 | tf_op jit(solution)/shard_map/reduce_scatter | solution.py:83
  218.1 1.9 copy_bitcast_fusion
  220.0 7.1 %all-to-all-start.1 = ((bf16[8,128,256]{1,2,0:T(8,128)(2,1)}), bf16[8,128,256]{1,2,0:T(8,128)(2,1)S(1)}, u32[]{:S(2)}, u32[]{:S(2)}) async-start(bf16[8,128,256]{1,2,0:T(8,128)(2,1)} %copy_bitcast_fusion), calls=%async_computation.2 | async-start | bytes 1048576 | tf_op jit(solution)/shard_map/all_to_all | solution.py:89
  227.1 8.2 %fusion.20 = bf16[128,7,128]{2,0,1:T(8,128)(2,1)S(1)} fusion(bf16[7,128,8192]{1,2,0:T(8,128)(2,1)} %fusion.1, bf16[8192,256]{1,0:T(8,128)(2,1)} %all-gather.3.cloned.1.call-done), kind=kOutput, calls=%fused_computation.30 | convolution fusion | flops 1879277568 | bytes 17006592 | tf_op jit(solution)/shard_map/hqk,kd->qhd/dot_general | solution.py:73
  235.3 0.0 copy-start.7
  235.3 0.2 copy.56
  235.5 0.6 gather_fusion
  236.1 8.9 %all-to-all-done.1 = bf16[8,128,256]{1,2,0:T(8,128)(2,1)S(1)} async-done(((bf16[8,128,256]{1,2,0:T(8,128)(2,1)}), bf16[8,128,256]{1,2,0:T(8,128)(2,1)S(1)}, u32[]{:S(2)}, u32[]{:S(2)}) %all-to-all-start.1) | async-done | bytes 524320 | tf_op jit(solution)/shard_map/all_to_all | solution.py:89
  245.1 0.1 reduce
  245.2 0.1 copy.67
  245.3 0.0 copy-start.2
  245.3 0.1 copy.68
  245.4 0.0 copy-start.3
  245.4 0.6 gather_fusion.2
  246.0 0.6 gather_fusion.1
  246.6 13.8 %all-gather = bf16[256,1152]{1,0:T(8,128)(2,1)S(1)} all-gather(bf16[32,1152]{1,0:T(8,128)(2,1)S(1)} %pad_maximum_fusion.1), channel_id=2, replica_groups=mesh['cz'=8,'cy'=8,'section'=2,'dp'=4] {'section','dp'}, dimensions={0}, use_global_device_ids=true | all-gather | bytes 663552 | tf_op jit(solution)/shard_map/all_gather | solution.py:101
  260.4 0.6 copy.57
  261.1 0.1 copy.70
  261.1 4.2 %convolution_convert_fusion = bf16[128,2560]{1,0:T(8,128)(2,1)} fusion(bf16[448,2560]{1,0:T(8,128)(2,1)S(1)} %copy-done, bf16[128,2304]{1,0:T(8,128)(2,1)S(1)} %bitcast.106, bf16[2304,448]{0,1:T(8,128)(2,1)} %param.18), kind=kOutput, calls=%fused_computation.23 | convolution fusion | flops 558227456 | bytes 5603328 | tf_op jit(solution)/shard_map/dot_general | solution.py:115
  265.4 3.8 %all-to-all-start.2 = ((bf16[8,16,2560]{2,1,0:T(8,128)(2,1)}), bf16[8,16,2560]{2,1,0:T(8,128)(2,1)S(1)}, u32[]{:S(2)}, u32[]{:S(2)}) async-start(bf16[8,16,2560]{2,1,0:T(8,128)(2,1)} %bitcast.103), calls=%async_computation.3 | async-start | bytes 1310720 | tf_op jit(solution)/shard_map/all_to_all | solution.py:114
  269.2 10.9 %all-to-all-done.2 = bf16[8,16,2560]{2,1,0:T(8,128)(2,1)S(1)} async-done(((bf16[8,16,2560]{2,1,0:T(8,128)(2,1)}), bf16[8,16,2560]{2,1,0:T(8,128)(2,1)S(1)}, u32[]{:S(2)}, u32[]{:S(2)}) %all-to-all-start.2) | async-done | bytes 655392 | tf_op jit(solution)/shard_map/all_to_all | solution.py:114
  280.1 0.1 convert_reduce_fusion
  280.2 0.1 reshape.222
  280.2 1.3 gather_fusion.3
  (17 shorter events, 0.1 us)
Async XLA Ops:
  7.2 254.0 %copy-start = (bf16[448,2560]{1,0:T(8,128)(2,1)S(1)}, bf16[448,2560]{1,0:T(8,128)(2,1)}, u32[]{:S(2)}) copy-start(bf16[448,2560]{1,0:T(8,128)(2,1)} %param.19) | copy-start | bytes 6881284
  7.2 83.1 %all-gather.3.cloned.1.call-start = ((), (), s32[]{:S(2)}) async-start(), calls=%async_computation.4 | async-start | bytes 4718592 | tf_op jit(solution)/shard_map/all_gather | solution.py:38
  35.0 183.1 %reduce-scatter.2.cloned.1.call-start = ((), (), s32[]{:S(2)}) async-start(), calls=%async_computation.5 | async-start | bytes 4718592 | tf_op jit(solution)/shard_map/reduce_scatter | solution.py:83
  103.4 12.7 %copy-start.4 = (bf16[1,128,896]{1,2,0:T(8,128)(2,1)S(1)}, bf16[1,128,896]{1,2,0:T(8,128)(2,1)}, u32[]{:S(2)}) copy-start(bf16[1,128,896]{1,2,0:T(8,128)(2,1)} %copy.46) | copy-start | bytes 688132
  116.1 13.4 %copy-start.1 = (bf16[8192,256]{1,0:T(8,128)(2,1)S(1)}, bf16[8192,256]{1,0:T(8,128)(2,1)}, u32[]{:S(2)}) copy-start(bf16[8192,256]{1,0:T(8,128)(2,1)} %all-gather.3.cloned.1.call-done) | copy-start | bytes 12582916
  129.5 19.4 %copy-start.5 = (bf16[1,128,896]{1,2,0:T(8,128)(2,1)S(1)}, bf16[1,128,896]{1,2,0:T(8,128)(2,1)}, u32[]{:S(2)}) copy-start(bf16[1,128,896]{1,2,0:T(8,128)(2,1)} %copy.44) | copy-start | bytes 688132
  158.8 2.4 copy-start.6
  220.0 25.1 %all-to-all-start.1 = ((bf16[8,128,256]{1,2,0:T(8,128)(2,1)}), bf16[8,128,256]{1,2,0:T(8,128)(2,1)S(1)}, u32[]{:S(2)}, u32[]{:S(2)}) async-start(bf16[8,128,256]{1,2,0:T(8,128)(2,1)} %copy_bitcast_fusion), calls=%async_computation.2 | async-start | bytes 1048576 | tf_op jit(solution)/shard_map/all_to_all | solution.py:89
  235.3 33.9 %copy-start.7 = (s32[1,1,64]{2,1,0:T(1,128)S(1)}, s32[1,1,64]{2,1,0:T(1,128)}, u32[]{:S(2)}) copy-start(s32[1,1,64]{2,1,0:T(1,128)} %param.17) | copy-start | bytes 772
  245.3 36.3 %copy-start.2 = (bf16[128,128]{1,0:T(8,128)(2,1)}, bf16[128,128]{1,0:T(8,128)(2,1)S(1)}, u32[]{:S(2)}) copy-start(bf16[128,128]{1,0:T(8,128)(2,1)S(1)} %copy.67) | copy-start | bytes 98308
  245.4 36.2 %copy-start.3 = (bf16[128,128]{1,0:T(8,128)(2,1)}, bf16[128,128]{1,0:T(8,128)(2,1)S(1)}, u32[]{:S(2)}) copy-start(bf16[128,128]{1,0:T(8,128)(2,1)S(1)} %copy.68) | copy-start | bytes 98308
  265.4 14.7 %all-to-all-start.2 = ((bf16[8,16,2560]{2,1,0:T(8,128)(2,1)}), bf16[8,16,2560]{2,1,0:T(8,128)(2,1)S(1)}, u32[]{:S(2)}, u32[]{:S(2)}) async-start(bf16[8,16,2560]{2,1,0:T(8,128)(2,1)} %bitcast.103), calls=%async_computation.3 | async-start | bytes 1310720 | tf_op jit(solution)/shard_map/all_to_all | solution.py:114
Sparse Core Ops, SparseCore 0:
  35.1 55.0 all-gather.2
  161.4 56.6 reduce-scatter.1
where the time goes:
time: 289 us; the launch traced here: 288 us
  waiting for transfers between devices  123 us (43%)
  matrix products  68.2 us (24%)
  blocking collectives  40.6 us (14%)
  other arithmetic  19.8 us (7%)
  between operations  14.3 us (5%)
  local copies, waits for them, and re-layouts  11.2 us (4%)
  starting transfers between devices  11 us (4%)
    reduce_scatter x1, waiting for transfers between devices, shards(): lax.psum_scatter(jnp.concatenate([key_part, value_part], axis=1).astype(j...  56.8 us
    all_gather x1, waiting for transfers between devices, shards(): lax.all_gather(lax.all_to_all(jnp.tile(own_pair, (ring_z, 1)), 'cz', 0, 0...  46.8 us
    all_to_all x1, blocking collectives, shards(): lax.all_to_all(jnp.tile(own_pair, (ring_z, 1)), 'cz', 0, 0, tiled=True)  26.8 us
    dot_general x1, matrix products, shards(): jnp.einsum('qhd,kd->hqk', grad_heads, value_all, preferred_element_type=j...  19.4 us
    all_gather x1, blocking collectives, shards(): lax.all_gather(chosen[None], ('section', 'dp'), axis=0, tiled=True)  13.8 us
    dot_general x1, matrix products, shards(): jnp.einsum('hqk,qhd->kd', probs_low, grad_heads, preferred_element_type=j...  13.4 us
    dot_general x1, matrix products, shards(): jnp.einsum('qhd,kd->hqk', query_heads, key_all, preferred_element_type=jn...  13.1 us
    reduce_sum x1, other arithmetic, shards(): summed = jnp.exp(masked_scores - running[:, :, None]).sum(axis=-1)  12.7 us
  transfers between devices with their start and end apart: 4, of which 4 were waited for; matrix products, arithmetic and copies ran while one was open for 6% of the time, Pallas kernels for 0%

commit v1 on v0

--- a/solution.py
+++ b/solution.py
@@ -35,11 +35,17 @@
     query_pos = query_first + jnp.arange(local_rows, dtype=jnp.int32)
     query_frames = lax.dynamic_slice_in_dim(frame_line, query_first, local_rows)
     own_pair = jnp.concatenate([key_vectors[0], value_vectors[0]], axis=1)
-    all_pairs = lax.all_gather(
-        lax.all_to_all(jnp.tile(own_pair, (ring_z, 1)), "cz", 0, 0, tiled=True),
-        "cy",
+    all_pairs = jnp.concatenate(
+        lax.all_to_all(
+            jnp.stack(
+                [lax.all_to_all(jnp.tile(own_pair, (ring_z, 1)), "cz", 0, 0, tiled=True)]
+                * lax.axis_size("cy")
+            ),
+            "cy",
+            0,
+            0,
+        ),
         axis=0,
-        tiled=True,
     )
     key_all = all_pairs[:, :HEAD_DIM]
     value_all = all_pairs[:, HEAD_DIM:]

time: 289 us -> 333 us (1.15)
  waiting for transfers between devices: 123 us -> 162 us
  starting transfers between devices: 11 us -> 17.8 us
    all_to_all x0 -> x1, waiting for transfers between devices: none -> 92.2 us  [shards(): lax.all_to_all(jnp.stack([lax.all_to_all(jnp.tile(own_pair, (ring_z, 1)),...]
    all_gather x1 -> x0, waiting for transfers between devices: 46.8 us -> none  [shards(): lax.all_gather(lax.all_to_all(jnp.tile(own_pair, (ring_z, 1)), 'cz', 0, 0...]
    reduce_scatter x1, waiting for transfers between devices: 56.8 us -> 49.8 us  [shards(): lax.psum_scatter(jnp.concatenate([key_part, value_part], axis=1).astype(j...]
    all_to_all x0 -> x1, starting transfers between devices: none -> 6.82 us  [shards(): lax.all_to_all(jnp.stack([lax.all_to_all(jnp.tile(own_pair, (ring_z, 1)),...]
  transfers between devices with their start and end apart: 4 -> 4, of which waited for: 4 -> 4; matrix products, arithmetic and copies ran while one was open for 6% -> 4% of each run, Pallas kernels for 0% -> 0%
where the time goes in v1:
time: 333 us; the launch traced here: 332 us
  waiting for transfers between devices  162 us (49%)
  matrix products  68.4 us (21%)
  blocking collectives  40.5 us (12%)
  other arithmetic  19 us (6%)
  starting transfers between devices  17.8 us (5%)
  between operations  14.3 us (4%)
  local copies, waits for them, and re-layouts  10.2 us (3%)
    all_to_all x1, waiting for transfers between devices, shards(): lax.all_to_all(jnp.stack([lax.all_to_all(jnp.tile(own_pair, (ring_z, 1)),...  92.2 us
    reduce_scatter x1, waiting for transfers between devices, shards(): lax.psum_scatter(jnp.concatenate([key_part, value_part], axis=1).astype(j...  49.8 us
    all_to_all x1, blocking collectives, shards(): lax.all_to_all(jnp.tile(own_pair, (ring_z, 1)), 'cz', 0, 0, tiled=True)  26.7 us
    dot_general x1, matrix products, shards(): jnp.einsum('qhd,kd->hqk', grad_heads, value_all, preferred_element_type=j...  19.8 us
    all_gather x1, blocking collectives, shards(): lax.all_gather(chosen[None], ('section', 'dp'), axis=0, tiled=True)  13.8 us
    dot_general x1, matrix products, shards(): jnp.einsum('hqk,qhd->kd', probs_low, grad_heads, preferred_element_type=j...  13.2 us
    dot_general x1, matrix products, shards(): jnp.einsum('qhd,kd->hqk', query_heads, key_all, preferred_element_type=jn...  13.1 us
    reduce_sum x1, other arithmetic, shards(): summed = jnp.exp(masked_scores - running[:, :, None]).sum(axis=-1)  12.7 us
  transfers between devices with their start and end apart: 4, of which 4 were waited for; matrix products, arithmetic and copies ran while one was open for 4% of the time, Pallas kernels for 0%

profile of v1, /device:TPU:1, one launch (start us, length us, event | category | flops | bytes accessed | tf_op | source)
XLA Modules:
  0.0 332.1 jit_solution(7447790130765332575)
XLA Ops:
  7.2 0.0 copy-start
  7.2 0.9 pad_maximum_fusion.2
  8.2 26.7 %all_to_all.29 = bf16[8,128,256]{2,1,0:T(8,128)(2,1)S(1)} all-to-all(bf16[8,128,256]{2,1,0:T(8,128)(2,1)S(1)} %tile.2), channel_id=1, replica_groups=mesh['cz'=8,'cy'=8,'section'=2,'dp'=4] {'cz'}, dimensions={0} | all-to-all | bytes 1048576 | tf_op jit(solution)/shard_map/all_to_all | solution.py:41
  34.9 2.2 stack.5
  37.1 6.8 %all-to-all-start.1 = ((bf16[8,1024,256]{2,1,0:T(8,128)(2,1)}), bf16[8,1024,256]{2,1,0:T(8,128)(2,1)}, u32[]{:S(2)}, u32[]{:S(2)}) async-start(bf16[8,1024,256]{2,1,0:T(8,128)(2,1)} %stack.5), calls=%async_computation.1 | async-start | bytes 8388608 | tf_op jit(solution)/shard_map/all_to_all | solution.py:39
  43.9 0.0 reduce-scatter.2.cloned.1.call-start
  43.9 0.0 copy-done.3
  43.9 0.8 copy.46
  44.8 0.9 copy.44
  45.6 0.0 copy-done.8
  45.6 0.0 copy-done.7
  45.7 2.8 compare_or_fusion
  48.5 92.2 %all-to-all-done.1 = bf16[8,1024,256]{2,1,0:T(8,128)(2,1)} async-done(((bf16[8,1024,256]{2,1,0:T(8,128)(2,1)}), bf16[8,1024,256]{2,1,0:T(8,128)(2,1)}, u32[]{:S(2)}, u32[]{:S(2)}) %all-to-all-start.1) | async-done | bytes 4194336 | tf_op jit(solution)/shard_map/all_to_all | solution.py:39
  140.7 13.1 %fusion.4 = (f32[7,128]{1,0:T(8,128)S(1)}, f32[8192,128,7]{1,0,2:T(8,128)}) fusion(pred[128,8192]{0,1:T(8,128)(4,1)S(1)} %compare_or_fusion, bf16[128,7,128]{0,2,1:T(8,128)(2,1)} %bitcast.114, bf16[8192,256]{1,0:T(8,128)(2,1)} %bitcast.8), kind=kOutput, calls=%fused_computation.12 | convolution fusion | flops 1901067392 | bytes 32738816 | tf_op jit(solution)/shard_map/qhd,kd->hqk/dot_general | solution.py:65
  153.9 12.7 %exponential_reduce_fusion = f32[7,128]{1,0:T(8,128)S(1)} fusion(f32[8192,128,7]{1,0,2:T(8,128)} %get-tuple-element.6, f32[7,128]{1,0:T(8,128)S(1)} %get-tuple-element.5, pred[128,8192]{0,1:T(8,128)(4,1)S(1)} %compare_or_fusion), kind=kLoop, calls=%fused_computation.11 | loop fusion | flops 29359232 | bytes 30415872 | tf_op jit(solution)/shard_map/reduce_sum | solution.py:70
  166.6 0.0 copy-done.5
  166.6 13.2 %fusion.13 = bf16[8192,128]{0,1:T(8,128)(2,1)S(1)} fusion(bf16[128,7,128]{0,2,1:T(8,128)(2,1)S(1)} %bitcast.112, f32[8192,128,7]{1,0,2:T(8,128)} %get-tuple-element.6, f32[7,128]{1,0:T(8,128)S(1)} %log_add_fusion, pred[128,8192]{0,1:T(8,128)(4,1)S(1)} %compare_or_fusion), kind=kOutput, calls=%fused_computation.19 | convolution fusion | flops 1909456896 | bytes 32738816 | tf_op jit(solution)/shard_map/hqk,qhd->kd/dot_general | solution.py:86
  179.8 0.0 copy-start.6
  179.8 19.8 %fusion.1 = bf16[7,128,8192]{1,2,0:T(8,128)(2,1)} fusion(f32[8192,128,7]{1,0,2:T(8,128)} %get-tuple-element.6, bf16[128,7,128]{0,2,1:T(8,128)(2,1)S(1)} %bitcast.113, f32[7,128]{1,0:T(8,128)S(1)} %bitcast.120, f32[7,128]{1,0:T(8,128)S(1)} %log_add_fusion, pred[128,8192]{0,1:T(8,128)(4,1)S(1)} %compare_or_fusion, bf16[8192,256]{1,0:T(8,128)(2,1)} %bitcast.8), kind=kOutput, calls=%fused_computation.6 | convolution fusion | flops 1923088384 | bytes 47422464 | tf_op jit(solution)/shard_map/qhd,kd->hqk/dot_general | solution.py:74
  199.6 9.9 %fusion.16 = bf16[8192,128]{0,1:T(8,128)(2,1)S(1)} fusion(bf16[7,128,8192]{1,2,0:T(8,128)(2,1)} %fusion.1, bf16[128,7,128]{0,2,1:T(8,128)(2,1)S(1)} %bitcast.115), kind=kOutput, calls=%fused_computation.20 | convolution fusion | flops 1881145344 | bytes 17006592 | tf_op jit(solution)/shard_map/hqk,qhd->kd/dot_general | solution.py:83
  209.5 0.0 copy-start.9
  209.5 2.4 pad_maximum_fusion
  211.9 0.0 reduce-scatter.2.cloned.1.call-update
  211.9 0.0 copy-done.9
  212.0 49.8 %reduce-scatter.2.cloned.1.call-done = bf16[1024,256]{0,1:T(8,128)(2,1)} async-done(((bf16[8192,256]{0,1:T(8,128)(2,1)}), bf16[1024,256]{0,1:T(8,128)(2,1)}) %reduce-scatter.2.cloned.1.call-update) | async-done | bytes 524304 | tf_op jit(solution)/shard_map/reduce_scatter | solution.py:89
  261.8 1.9 copy_bitcast_fusion
  263.7 7.1 %all-to-all-start.2 = ((bf16[8,128,256]{1,2,0:T(8,128)(2,1)}), bf16[8,128,256]{1,2,0:T(8,128)(2,1)S(1)}, u32[]{:S(2)}, u32[]{:S(2)}) async-start(bf16[8,128,256]{1,2,0:T(8,128)(2,1)} %copy_bitcast_fusion), calls=%async_computation.3 | async-start | bytes 1048576 | tf_op jit(solution)/shard_map/all_to_all | solution.py:95
  270.8 8.2 %fusion.20 = bf16[128,7,128]{2,0,1:T(8,128)(2,1)S(1)} fusion(bf16[7,128,8192]{1,2,0:T(8,128)(2,1)} %fusion.1, bf16[8192,256]{1,0:T(8,128)(2,1)} %bitcast.8), kind=kOutput, calls=%fused_computation.30 | convolution fusion | flops 1879277568 | bytes 17006592 | tf_op jit(solution)/shard_map/hqk,kd->qhd/dot_general | solution.py:79
  279.0 0.0 copy-start.10
  279.0 0.2 copy.56
  279.2 0.6 gather_fusion
  279.8 8.9 %all-to-all-done.2 = bf16[8,128,256]{1,2,0:T(8,128)(2,1)S(1)} async-done(((bf16[8,128,256]{1,2,0:T(8,128)(2,1)}), bf16[8,128,256]{1,2,0:T(8,128)(2,1)S(1)}, u32[]{:S(2)}, u32[]{:S(2)}) %all-to-all-start.2) | async-done | bytes 524320 | tf_op jit(solution)/shard_map/all_to_all | solution.py:95
  288.8 0.1 reduce
  288.9 0.1 copy.67
  289.0 0.0 copy-start.1
  289.0 0.1 copy.68
  289.1 0.0 copy-start.2
  289.1 0.6 gather_fusion.2
  289.7 0.6 gather_fusion.1
  290.3 13.8 %all-gather = bf16[256,1152]{1,0:T(8,128)(2,1)S(1)} all-gather(bf16[32,1152]{1,0:T(8,128)(2,1)S(1)} %pad_maximum_fusion.1), channel_id=2, replica_groups=mesh['cz'=8,'cy'=8,'section'=2,'dp'=4] {'section','dp'}, dimensions={0}, use_global_device_ids=true | all-gather | bytes 663552 | tf_op jit(solution)/shard_map/all_gather | solution.py:107
  304.1 0.6 copy.57
  304.7 0.1 copy.70
  304.8 4.2 %convolution_convert_fusion = bf16[128,2560]{1,0:T(8,128)(2,1)} fusion(bf16[448,2560]{1,0:T(8,128)(2,1)S(1)} %copy-done, bf16[128,2304]{1,0:T(8,128)(2,1)S(1)} %bitcast.107, bf16[2304,448]{0,1:T(8,128)(2,1)} %param.18), kind=kOutput, calls=%fused_computation.23 | convolution fusion | flops 558227456 | bytes 5603328 | tf_op jit(solution)/shard_map/dot_general | solution.py:121
  309.0 3.8 %all-to-all-start.3 = ((bf16[8,16,2560]{2,1,0:T(8,128)(2,1)}), bf16[8,16,2560]{2,1,0:T(8,128)(2,1)S(1)}, u32[]{:S(2)}, u32[]{:S(2)}) async-start(bf16[8,16,2560]{2,1,0:T(8,128)(2,1)} %bitcast.104), calls=%async_computation.4 | async-start | bytes 1310720 | tf_op jit(solution)/shard_map/all_to_all | solution.py:120
  312.9 10.9 %all-to-all-done.3 = bf16[8,16,2560]{2,1,0:T(8,128)(2,1)S(1)} async-done(((bf16[8,16,2560]{2,1,0:T(8,128)(2,1)}), bf16[8,16,2560]{2,1,0:T(8,128)(2,1)S(1)}, u32[]{:S(2)}, u32[]{:S(2)}) %all-to-all-start.3) | async-done | bytes 655392 | tf_op jit(solution)/shard_map/all_to_all | solution.py:120
  323.7 0.1 convert_reduce_fusion
  323.8 0.1 reshape.229
  323.9 1.3 gather_fusion.3
  (23 shorter events, 0.1 us)
Async XLA Ops:
  7.2 297.6 %copy-start = (bf16[448,2560]{1,0:T(8,128)(2,1)S(1)}, bf16[448,2560]{1,0:T(8,128)(2,1)}, u32[]{:S(2)}) copy-start(bf16[448,2560]{1,0:T(8,128)(2,1)} %param.19) | copy-start | bytes 6881284
  7.2 36.7 %copy-start.3 = (bf16[1,128,896]{2,1,0:T(8,128)(2,1)S(1)}, bf16[1,128,896]{2,1,0:T(8,128)(2,1)}, u32[]{:S(2)}) copy-start(bf16[1,128,896]{2,1,0:T(8,128)(2,1)} %param.13) | copy-start | bytes 688132
  7.2 37.6 %copy-start.4 = (bf16[1,128,896]{2,1,0:T(8,128)(2,1)S(1)}, bf16[1,128,896]{2,1,0:T(8,128)(2,1)}, u32[]{:S(2)}) copy-start(bf16[1,128,896]{2,1,0:T(8,128)(2,1)} %param.10) | copy-start | bytes 688132
  7.2 38.4 %copy-start.8 = (f32[1,7,128]{2,0,1:T(1,128)S(1)}, f32[1,7,128]{2,0,1:T(1,128)}, u32[]{:S(2)}) copy-start(f32[1,7,128]{2,0,1:T(1,128)} %param.14) | copy-start | bytes 10756
  7.2 38.4 %copy-start.7 = (s32[1,8192]{1,0:T(1,128)S(1)}, s32[1,8192]{1,0:T(1,128)}, u32[]{:S(2)}) copy-start(s32[1,8192]{1,0:T(1,128)} %param.15) | copy-start | bytes 98308
  37.1 103.7 %all-to-all-start.1 = ((bf16[8,1024,256]{2,1,0:T(8,128)(2,1)}), bf16[8,1024,256]{2,1,0:T(8,128)(2,1)}, u32[]{:S(2)}, u32[]{:S(2)}) async-start(bf16[8,1024,256]{2,1,0:T(8,128)(2,1)} %stack.5), calls=%async_computation.1 | async-start | bytes 8388608 | tf_op jit(solution)/shard_map/all_to_all | solution.py:39
  43.9 217.9 %reduce-scatter.2.cloned.1.call-start = ((), (), s32[]{:S(2)}) async-start(), calls=%async_computation.5 | async-start | bytes 4718592 | tf_op jit(solution)/shard_map/reduce_scatter | solution.py:89
  153.9 12.7 %copy-start.5 = (bf16[1,128,896]{1,2,0:T(8,128)(2,1)S(1)}, bf16[1,128,896]{1,2,0:T(8,128)(2,1)}, u32[]{:S(2)}) copy-start(bf16[1,128,896]{1,2,0:T(8,128)(2,1)} %copy.46) | copy-start | bytes 688132
  179.8 19.8 %copy-start.6 = (bf16[1,128,896]{1,2,0:T(8,128)(2,1)S(1)}, bf16[1,128,896]{1,2,0:T(8,128)(2,1)}, u32[]{:S(2)}) copy-start(bf16[1,128,896]{1,2,0:T(8,128)(2,1)} %copy.44) | copy-start | bytes 688132
  209.5 2.4 copy-start.9
  263.7 25.1 %all-to-all-start.2 = ((bf16[8,128,256]{1,2,0:T(8,128)(2,1)}), bf16[8,128,256]{1,2,0:T(8,128)(2,1)S(1)}, u32[]{:S(2)}, u32[]{:S(2)}) async-start(bf16[8,128,256]{1,2,0:T(8,128)(2,1)} %copy_bitcast_fusion), calls=%async_computation.3 | async-start | bytes 1048576 | tf_op jit(solution)/shard_map/all_to_all | solution.py:95
  279.0 33.8 %copy-start.10 = (s32[1,1,64]{2,1,0:T(1,128)S(1)}, s32[1,1,64]{2,1,0:T(1,128)}, u32[]{:S(2)}) copy-start(s32[1,1,64]{2,1,0:T(1,128)} %param.17) | copy-start | bytes 772
  289.0 36.3 %copy-start.1 = (bf16[128,128]{1,0:T(8,128)(2,1)}, bf16[128,128]{1,0:T(8,128)(2,1)S(1)}, u32[]{:S(2)}) copy-start(bf16[128,128]{1,0:T(8,128)(2,1)S(1)} %copy.67) | copy-start | bytes 98308
  289.1 36.1 %copy-start.2 = (bf16[128,128]{1,0:T(8,128)(2,1)}, bf16[128,128]{1,0:T(8,128)(2,1)S(1)}, u32[]{:S(2)}) copy-start(bf16[128,128]{1,0:T(8,128)(2,1)S(1)} %copy.68) | copy-start | bytes 98308
  309.0 14.7 %all-to-all-start.3 = ((bf16[8,16,2560]{2,1,0:T(8,128)(2,1)}), bf16[8,16,2560]{2,1,0:T(8,128)(2,1)S(1)}, u32[]{:S(2)}, u32[]{:S(2)}) async-start(bf16[8,16,2560]{2,1,0:T(8,128)(2,1)} %bitcast.104), calls=%async_computation.4 | async-start | bytes 1310720 | tf_op jit(solution)/shard_map/all_to_all | solution.py:120
Sparse Core Ops, SparseCore 0:
  212.1 49.6 reduce-scatter.1
